TPU v7x, 32 devices: a whole 2x2x4 slice. The times are simulated.
32 devices in a mesh: rep: 8 (over z, x), tile: 4 (over y, core).
Axes of the slice: x: 2, y: 2, z: 4, core: 2. Of those that a mesh axis runs over, the one named last changes fastest.
Arguments:
- features: bfloat16 [16, 48, 72, 1536], P('rep', 'tile'), may hold values from -6 to 6
- conv_out: bfloat16 [16, 48, 72, 256], P('rep', 'tile'), may hold values from -6 to 6
- conv_weight: bfloat16 [9, 1536, 256], replicated, may hold values from -0.0546875 to 0.0546875
- norm_gain_vector: float32 [256], replicated, may hold values from 0.5 to 1.5
- norm_shift_vector: float32 [256], replicated, may hold values from -3 to 3
- class_map: float32 [3, 256], replicated, may hold values from -3 to 3
- labels: int32 [16, 48, 72], P('rep', 'tile'), may hold values from 0 to 2
- class_weight: int32 [3], replicated, may hold values from 1 to 39
Outputs:
- grad_features: bfloat16 [16, 48, 72, 1536], P('rep', 'tile')
- grad_weight: float32 [1536, 9, 256], P(('rep', 'tile'))
- grad_gain: float32 [256], replicated
- grad_shift: float32 [256], replicated
- grad_class: float32 [3, 256], replicated
- loss: float32 [], replicated
All inputs are finite; a program needn't handle non-finite values.
Results may differ from a plain program's by a relative error of at most 0.0049.
Values may be sent and summed in bfloat16 or wider, within the bound.
No kernel may reach another device: no remote copies, remote signals or barrier semaphores. Data moves between devices by JAX's collectives and lax.ppermute only.
A program may use at most 256 MiB of HBM per device.

v0:
```python
import jax
import jax.numpy as jnp
from jax import lax
from jax.sharding import PartitionSpec as P

IMG_DEV = 2
H = 48
W = 72
RATE = 12


def padded(x, sides, width):
    for axis, dim in sides:
        size, length = (lax.axis_size(axis), x.shape[dim])
        up = [(i, (i + 1) % size) for i in range(size - 1)]
        down = [(j, i) for i, j in up]
        last = lax.slice_in_dim(x, length - width, length, axis=dim)
        first = lax.slice_in_dim(x, 0, width, axis=dim)
        before = lax.ppermute(last, axis, up)
        after = lax.ppermute(first, axis, down)
        x = jnp.concatenate([before, x, after], axis=dim)
    return x


def body(
    features,
    conv_out,
    conv_weight,
    norm_gain_vector,
    norm_shift_vector,
    class_map,
    labels,
    class_weight,
):
    highest = lax.Precision.HIGHEST
    images, tile_rows, columns, in_chans = features.shape
    out_chans = conv_out.shape[3]
    local_pix = images * tile_rows * columns
    per_replica_part = IMG_DEV * H * W
    all_pix = lax.axis_size("rep") * per_replica_part
    yvals = conv_out.astype(jnp.float32).reshape(local_pix, out_chans)
    column_sum = lax.psum(jnp.sum(yvals, 0), "tile")
    centre_offset = yvals - column_sum / per_replica_part
    variance = lax.psum(jnp.sum(centre_offset * centre_offset, 0), "tile") / per_replica_part
    inverse_deviation = lax.rsqrt(variance + 1e-05)
    normalized_input = centre_offset * inverse_deviation
    preactivation_values = norm_gain_vector * normalized_input + norm_shift_vector
    zvals = jnp.maximum(preactivation_values, 0.0)
    logits = jnp.dot(zvals, class_map.T, precision=highest)
    onehot = (
        labels.reshape(local_pix, 1) == jnp.arange(class_map.shape[0], dtype=jnp.int32)
    ).astype(jnp.float32)
    weights_pix = jnp.sum(onehot * class_weight.astype(jnp.float32), -1)
    top_val = jnp.max(logits, -1, keepdims=True)
    log_total = top_val[:, 0] + jnp.log(jnp.sum(jnp.exp(logits - top_val), -1))
    cross = log_total - jnp.sum(onehot * logits, -1)
    weight_total, loss_total = lax.psum(
        (jnp.sum(weights_pix), jnp.sum(weights_pix * cross)), ("rep", "tile")
    )
    mean_weight = weight_total / all_pix
    loss = loss_total / mean_weight / all_pix
    probs = jnp.exp(logits - log_total[:, None])
    grad_logit = (weights_pix / mean_weight)[:, None] * (probs - onehot)
    class_local_slice = jnp.dot(grad_logit.T, zvals, precision=highest)
    grad_z = jnp.dot(grad_logit, class_map, precision=highest)
    preactivation_gradient = jnp.where(preactivation_values > 0, grad_z, 0.0)
    first_gradient_sum, second_gradient_sum, class_tile = lax.psum(
        (
            jnp.sum(preactivation_gradient, 0),
            jnp.sum(preactivation_gradient * normalized_input, 0),
            class_local_slice,
        ),
        "tile",
    )
    grad_shift, grad_gain, grad_class = lax.psum(
        (first_gradient_sum, second_gradient_sum, class_tile), "rep"
    )
    normalized_output_gradient = (
        norm_gain_vector
        * inverse_deviation
        * (
            preactivation_gradient
            - first_gradient_sum / per_replica_part
            - normalized_input * second_gradient_sum / per_replica_part
        )
    ).astype(jnp.bfloat16)
    normalized_output_gradient = normalized_output_gradient.reshape(
        images, tile_rows, columns, out_chans
    )
    extended = padded(normalized_output_gradient, (("tile", 1),), RATE)
    extended = jnp.pad(extended, ((0, 0), (0, 0), (RATE, RATE), (0, 0)))
    shifted_list = []
    for tap_index in range(9):
        row_off = RATE - (tap_index // 3 - 1) * RATE
        col_off = RATE - (tap_index % 3 - 1) * RATE
        piece = extended[:, row_off : row_off + tile_rows, col_off : col_off + columns, :]
        shifted_list.append(piece.reshape(local_pix, out_chans))
    accum_grad = jnp.zeros((local_pix, in_chans), jnp.float32)
    for tap_index in range(9):
        accum_grad = accum_grad + lax.dot_general(
            shifted_list[tap_index],
            conv_weight[tap_index],
            (((1,), (1,)), ((), ())),
            preferred_element_type=jnp.float32,
        )
    grad_features = accum_grad.astype(jnp.bfloat16).reshape(images, tile_rows, columns, in_chans)
    flat_x = features.reshape(local_pix, in_chans)
    parts_list = [
        lax.dot_general(
            flat_x, shifted, (((0,), (0,)), ((), ())), preferred_element_type=jnp.float32
        )
        for shifted in shifted_list
    ]
    grad_weight = lax.psum_scatter(
        jnp.stack(parts_list, 1), ("rep", "tile"), scatter_dimension=0, tiled=True
    )
    return (grad_features, grad_weight, grad_gain, grad_shift, grad_class, loss)


def solution(mesh):
    in_specs = (
        P("rep", "tile", None, None),
        P("rep", "tile", None, None),
        P(),
        P(),
        P(),
        P(),
        P("rep", "tile", None),
        P(),
    )
    out_specs = (P("rep", "tile", None, None), P(("rep", "tile"), None, None), P(), P(), P(), P())
    return jax.shard_map(body, mesh=mesh, in_specs=in_specs, out_specs=out_specs, check_vma=False)
```

profile of v0, /device:TPU:0, one launch (start us, length us, event | category | flops | bytes accessed | tf_op | source)
XLA Modules:
  0.0 405.0 jit_solution(10787423601491690530)
XLA Ops:
  8.7 8.4 %psum.70 = f32[256]{0:T(256)S(1)} all-reduce(f32[256]{0:T(256)S(1)} %convert_reduce_fusion), channel_id=1, replica_groups=mesh['rep'=8,'tile'=4] {'tile'}, use_global_device_ids=true, to_apply=%region_1.0 | all-reduce | flops 256 | bytes 2048 | tf_op jit(solution)/shard_map/psum | solution.py:42
  18.5 5.8 %psum.71 = f32[256]{0:T(256)S(1)} all-reduce(f32[256]{0:T(256)S(1)} %multiply_reduce_fusion.1), channel_id=1, replica_groups=mesh['rep'=8,'tile'=4] {'tile'}, use_global_device_ids=true, to_apply=%region_3.0 | all-reduce | flops 256 | bytes 2048 | tf_op jit(solution)/shard_map/psum | solution.py:44
  27.7 2.5 fusion.63
  31.5 39.9 %all-reduce.1 = (f32[]{:T(128)}, f32[]{:T(128)}) all-reduce(f32[]{:T(128)} %get-tuple-element.31, f32[]{:T(128)} %get-tuple-element.40), channel_id=1, replica_groups=mesh['rep'=8,'tile'=4] {'rep','tile'}, use_global_device_ids=true, to_apply=%region_6.0 | all-reduce | flops 2 | bytes 16 | tf_op jit(solution)/shard_map/psum | solution.py:57
  73.1 4.6 %fusion.61 = (f32[256]{0:T(256)S(1)}, f32[256]{0:T(256)S(1)}, f32[1728,256]{1,0:T(8,128)}) fusion(f32[256]{0:T(256)S(1)} %get-tuple-element.49, f32[256]{0:T(256)S(1)} %broadcast_multiply_fusion.1, bf16[2,12,72,256]{3,2,1,0:T(8,128)(2,1)} %param.9, f32[3,256]{1,0:T(4,128)S(1)} %copy-done, f32[1728,3]{0,1:T(4,128)S(1)} %get-tuple-element.51, ...), kind=kOutput, calls=%fused_computation.92 | convolution fusion | flops 20374336 | bytes 4474368 | tf_op jit(solution)/shard_map/dot_general | solution.py:65
  77.6 6.9 %all-reduce.3 = (f32[256]{0:T(256)S(1)}, f32[256]{0:T(256)S(1)}, f32[3,256]{1,0:T(4,128)S(1)}) all-reduce(f32[256]{0:T(256)S(1)} %get-tuple-element.25, f32[256]{0:T(256)S(1)} %get-tuple-element.24, f32[3,256]{1,0:T(4,128)S(1)} %fusion.16), channel_id=1, replica_groups=mesh['rep'=8,'tile'=4] {'tile'}, use_global_device_ids=true, to_apply=%region_12.13 | all-reduce | flops 1280 | bytes 10240 | tf_op jit(solution)/shard_map/psum | solution.py:67
  84.5 2.3 multiply_convert_fusion
  86.9 1.5 collective-permute-start
  90.4 3.8 collective-permute-done.1
  94.2 1.8 fusion.5
  96.1 2.8 fusion.14
  98.9 2.8 fusion.13
  101.7 2.8 fusion.12
  104.4 2.8 fusion.11
  107.2 2.8 fusion.10
  110.0 2.8 fusion.9
  112.7 2.7 fusion.8
  115.5 2.8 fusion.7
  118.3 2.8 fusion.6
  121.0 19.0 %copy.18 = f32[1536,9,256]{2,1,0:T(8,128)} copy(f32[1536,9,256]{0,2,1:T(8,128)} %fusion.6) | data formatting | bytes 28311552 | tf_op jit(solution)/shard_map/stack | solution.py:115
  140.7 21.3 %all-reduce.2 = (f32[256]{0:T(256)}, f32[256]{0:T(256)}, f32[3,256]{1,0:T(4,128)}) all-reduce(f32[256]{0:T(256)S(1)} %get-tuple-element.37, f32[256]{0:T(256)S(1)} %get-tuple-element.38, f32[3,256]{1,0:T(4,128)S(1)} %get-tuple-element.39), channel_id=1, replica_groups=mesh['rep'=8,'tile'=4] {'rep'}, use_global_device_ids=true, to_apply=%region_14.15 | all-reduce | flops 1280 | bytes 10240 | tf_op jit(solution)/shard_map/psum | solution.py:75
  162.0 7.7 %fusion.33 = f32[1728,1536]{1,0:T(8,128)} fusion(bf16[1728,256]{1,0:T(8,128)(2,1)S(1)} %multiply_convert_fusion, bf16[9,1536,256]{2,1,0:T(8,128)(2,1)} %param.10), kind=kOutput, calls=%fused_computation.52 | convolution fusion | flops 1358954496 | bytes 12288000 | tf_op jit(solution)/shard_map/dot_general | solution.py:100
  170.3 8.2 %fusion.26 = f32[1728,1536]{1,0:T(8,128)} fusion(bf16[1728,256]{1,0:T(8,128)(2,1)S(1)} %bitcast.174, bf16[9,1536,256]{2,1,0:T(8,128)(2,1)} %param.10), kind=kOutput, calls=%fused_computation.45 | convolution fusion | flops 1358954496 | bytes 12288000 | tf_op jit(solution)/shard_map/dot_general | solution.py:100
  178.5 6.4 %fusion.29 = f32[1728,1536]{1,0:T(8,128)} fusion(bf16[1728,256]{1,0:T(8,128)(2,1)S(1)} %bitcast.173, bf16[9,1536,256]{2,1,0:T(8,128)(2,1)S(1)} %bitcast.167), kind=kOutput, calls=%fused_computation.48 | convolution fusion | flops 1358954496 | bytes 12288000 | tf_op jit(solution)/shard_map/dot_general | solution.py:100
  184.9 6.3 %fusion.31 = f32[1728,1536]{1,0:T(8,128)} fusion(bf16[1728,256]{1,0:T(8,128)(2,1)S(1)} %bitcast.172, bf16[9,1536,256]{2,1,0:T(8,128)(2,1)S(1)} %bitcast.167), kind=kOutput, calls=%fused_computation.50 | convolution fusion | flops 1358954496 | bytes 12288000 | tf_op jit(solution)/shard_map/dot_general | solution.py:100
  191.2 6.3 %fusion.35 = f32[1728,1536]{1,0:T(8,128)} fusion(bf16[1728,256]{1,0:T(8,128)(2,1)S(1)} %bitcast.171, bf16[9,1536,256]{2,1,0:T(8,128)(2,1)S(1)} %bitcast.167), kind=kOutput, calls=%fused_computation.54 | convolution fusion | flops 1358954496 | bytes 12288000 | tf_op jit(solution)/shard_map/dot_general | solution.py:100
  197.6 5.7 %fusion.37 = f32[1728,1536]{1,0:T(8,128)} fusion(bf16[1728,256]{1,0:T(8,128)(2,1)S(1)} %bitcast.170, bf16[9,1536,256]{2,1,0:T(8,128)(2,1)S(1)} %bitcast.167), kind=kOutput, calls=%fused_computation.56 | convolution fusion | flops 1358954496 | bytes 12288000 | tf_op jit(solution)/shard_map/dot_general | solution.py:100
  203.3 5.6 %fusion.41 = f32[1728,1536]{1,0:T(8,128)} fusion(bf16[1728,256]{1,0:T(8,128)(2,1)S(1)} %bitcast.169, bf16[9,1536,256]{2,1,0:T(8,128)(2,1)S(1)} %bitcast.167), kind=kOutput, calls=%fused_computation.60 | convolution fusion | flops 1358954496 | bytes 12288000 | tf_op jit(solution)/shard_map/dot_general | solution.py:100
  209.0 6.2 %fusion.39 = f32[1728,1536]{1,0:T(8,128)} fusion(bf16[1728,256]{1,0:T(8,128)(2,1)S(1)} %bitcast.164, bf16[9,1536,256]{2,1,0:T(8,128)(2,1)S(1)} %bitcast.167), kind=kOutput, calls=%fused_computation.58 | convolution fusion | flops 1358954496 | bytes 12288000 | tf_op jit(solution)/shard_map/dot_general | solution.py:100
  215.1 30.1 %add_convert_fusion = bf16[1728,1536]{1,0:T(8,128)(2,1)} fusion(f32[1728,1536]{1,0:T(8,128)} %fusion.26, f32[1728,1536]{1,0:T(8,128)} %fusion.29, f32[1728,1536]{1,0:T(8,128)} %fusion.31, f32[1728,1536]{1,0:T(8,128)} %fusion.33, f32[1728,1536]{1,0:T(8,128)} %fusion.35, f32[1728,1536]{1,0:T(8,128)} %fusion.37, f32[1728,1536]{1,0:T(8,128)} %fusion.41, ...), kind=kOutput, calls=%fused_computation.2 | convolution fusion | flops 1382842368 | bytes 91914240 | tf_op jit(solution)/shard_map/dot_general | solution.py:100
  245.2 149.6 %reduce-scatter.2.cloned.1.call-done = f32[48,9,256]{2,1,0:T(8,128)} async-done(((f32[1536,9,256]{2,1,0:T(8,128)}), f32[48,9,256]{2,1,0:T(8,128)}) %reduce-scatter.2.cloned.1.call-update) | async-done | bytes 442384 | tf_op jit(solution)/shard_map/reduce_scatter | solution.py:114
  394.8 2.2 copy.19
  (44 shorter events, 11.4 us)
Async XLA Ops:
  7.2 20.6 %copy-start = (f32[3,256]{1,0:T(4,128)S(1)}, f32[3,256]{1,0:T(4,128)}, u32[]{:S(2)}) copy-start(f32[3,256]{1,0:T(4,128)} %param.13) | copy-start | bytes 9220
  7.2 64.9 %copy-start.6 = (f32[256]{0:T(256)S(1)}, f32[256]{0:T(256)}, u32[]{:S(2)}) copy-start(f32[256]{0:T(256)} %param.11) | copy-start | bytes 3076
  7.2 64.9 %copy-start.7 = (f32[256]{0:T(256)S(1)}, f32[256]{0:T(256)}, u32[]{:S(2)}) copy-start(f32[256]{0:T(256)} %param.12) | copy-start | bytes 3076
  7.2 387.6 %reduce-scatter.2.cloned.1.call-start = ((), (), s32[]{:S(2)}) async-start(), calls=%async_computation.1 | async-start | bytes 25952256 | tf_op jit(solution)/shard_map/reduce_scatter | solution.py:114
  73.1 23.0 %slice-start = ((s8[5308416]{0:T(1024)(128)(4,1)}), s8[1114112]{0:T(1024)(128)(4,1)S(1)}, s32[]{:S(2)}) async-start(s8[5308416]{0:T(1024)(128)(4,1)} %bitcast.158), calls=%async_computation.2 | async-start | bytes 2228224
  84.5 11.5 %slice-start.1 = ((s8[5308416]{0:T(1024)(128)(4,1)}), s8[4194304]{0:T(1024)(128)(4,1)S(1)}, s32[]{:S(2)}) async-start(s8[5308416]{0:T(1024)(128)(4,1)} %bitcast.158), calls=%async_computation.3 | async-start | bytes 8388608
  86.9 3.5 collective-permute-start
  88.4 5.8 %collective-permute-start.1 = (bf16[2,12,72,256]{3,2,1,0:T(8,128)(2,1)S(1)}, bf16[2,12,72,256]{3,2,1,0:T(8,128)(2,1)S(1)}, u32[]{:S(2)}, u32[]{:S(2)}) collective-permute-start(bf16[2,12,72,256]{3,2,1,0:T(8,128)(2,1)S(1)} %bitcast.161), channel_id=1, source_target_pairs={{1,0},{2,1},{3,2},{5,4},{6,5},{7,6},{9,8},{10,9},{11,10},{13,12},{... | collective-permute-start | bytes 2654216 | tf_op jit(solution)/shard_map/ppermute | solution.py:20
  90.4 25.1 %copy-start.4 = (bf16[2,12,72,256]{3,2,1,0:T(8,128)(2,1)}, bf16[2,12,72,256]{3,2,1,0:T(8,128)(2,1)S(1)}, u32[]{:S(2)}) copy-start(bf16[2,12,72,256]{3,2,1,0:T(8,128)(2,1)S(1)} %collective-permute-done) | copy-start | bytes 2654212
  96.0 22.2 %copy-start.2 = (bf16[2,36,96,256]{3,2,1,0:T(8,128)(2,1)}, bf16[2,36,96,256]{3,2,1,0:T(8,128)(2,1)S(1)}, u32[]{:S(2)}) copy-start(bf16[2,36,96,256]{3,2,1,0:T(8,128)(2,1)S(1)} %fusion.5) | copy-start | bytes 10616836
  162.0 7.7 %copy-start.3 = (bf16[2,36,96,256]{3,2,1,0:T(8,128)(2,1)S(1)}, bf16[2,36,96,256]{3,2,1,0:T(8,128)(2,1)}, u32[]{:S(2)}) copy-start(bf16[2,36,96,256]{3,2,1,0:T(8,128)(2,1)} %copy-done.2) | copy-start | bytes 10616836
  169.7 8.8 %slice-start.2 = ((s8[7077888]{0:T(1024)(128)(4,1)}), s8[2883584]{0:T(1024)(128)(4,1)S(1)}, s32[]{:S(2)}) async-start(s8[7077888]{0:T(1024)(128)(4,1)} %bitcast.166), calls=%async_computation.4 | async-start | bytes 5767168
  170.3 8.2 %slice-start.3 = ((s8[7077888]{0:T(1024)(128)(4,1)}), s8[4194304]{0:T(1024)(128)(4,1)S(1)}, s32[]{:S(2)}) async-start(s8[7077888]{0:T(1024)(128)(4,1)} %bitcast.166), calls=%async_computation.5 | async-start | bytes 8388608
  208.9 6.2 %copy-start.5 = (bf16[2,12,72,256]{3,2,1,0:T(8,128)(2,1)S(1)}, bf16[2,12,72,256]{3,2,1,0:T(8,128)(2,1)}, u32[]{:S(2)}) copy-start(bf16[2,12,72,256]{3,2,1,0:T(8,128)(2,1)} %copy-done.4) | copy-start | bytes 2654212
  215.1 181.9 %copy-start.1 = (f32[3,256]{1,0:T(4,128)S(1)}, f32[3,256]{1,0:T(4,128)}, u32[]{:S(2)}) copy-start(f32[3,256]{1,0:T(4,128)} %param.13) | copy-start | bytes 9220
Sparse Core Ops, SparseCore 0:
  140.1 254.6 reduce-scatter.1
where the time goes:
time: 406 us; the launch traced here: 405 us
  waiting for transfers between devices  154 us (38%)
  matrix products  116 us (29%)
  blocking collectives  82.2 us (20%)
  local copies, waits for them, and re-layouts  22.6 us (6%)
  between operations  16.6 us (4%)
  other arithmetic  11.1 us (3%)
    reduce_scatter x1, waiting for transfers between devices, body(): lax.psum_scatter(jnp.stack(parts_list, 1), ('rep', 'tile'), scatter_dimen...  150 us
    dot_general x9, matrix products, body(): lax.dot_general(shifted_list[tap_index], conv_weight[tap_index], (((1,),...  82.6 us
    psum x1, blocking collectives, body(): lax.psum((jnp.sum(weights_pix), jnp.sum(weights_pix * cross)), ('rep', 't...  39.9 us
    dot_general x9, matrix products, body(): lax.dot_general(flat_x, shifted, (((0,), (0,)), ((), ())), preferred_elem...  25 us
    psum x1, blocking collectives, body(): lax.psum((first_gradient_sum, second_gradient_sum, class_tile), 'rep')  21.3 us
    another operation x1, local copies, waits for them, and re-layouts, body(): jnp.stack(parts_list, 1)  19 us
    psum x1, blocking collectives, body(): column_sum = lax.psum(jnp.sum(yvals, 0), 'tile')  8.36 us
  transfers between devices with their start and end apart: 3, of which 3 were waited for; matrix products, arithmetic and copies ran while one was open for 21% of the time, Pallas kernels for 0%

commit v1 on v0

--- a/solution.py
+++ b/solution.py
@@ -2,6 +2,7 @@
 import jax.numpy as jnp
 from jax import lax
 from jax.sharding import PartitionSpec as P
+from jax.lax import all_gather
 
 IMG_DEV = 2
 H = 48
@@ -39,7 +40,8 @@
     per_replica_part = IMG_DEV * H * W
     all_pix = lax.axis_size("rep") * per_replica_part
     yvals = conv_out.astype(jnp.float32).reshape(local_pix, out_chans)
-    column_sum = lax.psum(jnp.sum(yvals, 0), "tile")
+    vec = jnp.sum(yvals, 0)
+    column_sum = jnp.sum(all_gather(vec, axis_name="tile"), 0)
     centre_offset = yvals - column_sum / per_replica_part
     variance = lax.psum(jnp.sum(centre_offset * centre_offset, 0), "tile") / per_replica_part
     inverse_deviation = lax.rsqrt(variance + 1e-05)

time: 406 us -> 405 us (level)
    psum x1 -> x0, blocking collectives: 8.36 us -> none  [body(): column_sum = lax.psum(jnp.sum(yvals, 0), 'tile')]
    all_gather x0 -> x1, blocking collectives: none -> 6 us  [body(): column_sum = jnp.sum(all_gather(vec, axis_name='tile'), 0)]
where the time goes in v1:
time: 405 us; the launch traced here: 404 us
  waiting for transfers between devices  154 us (38%)
  matrix products  116 us (29%)
  blocking collectives  81.6 us (20%)
  local copies, waits for them, and re-layouts  22.6 us (6%)
  between operations  16.6 us (4%)
  other arithmetic  11.1 us (3%)
    reduce_scatter x1, waiting for transfers between devices, body(): lax.psum_scatter(jnp.stack(parts_list, 1), ('rep', 'tile'), scatter_dimen...  150 us
    dot_general x9, matrix products, body(): lax.dot_general(shifted_list[tap_index], conv_weight[tap_index], (((1,),...  82.6 us
    psum x1, blocking collectives, body(): lax.psum((jnp.sum(weights_pix), jnp.sum(weights_pix * cross)), ('rep', 't...  39.8 us
    dot_general x9, matrix products, body(): lax.dot_general(flat_x, shifted, (((0,), (0,)), ((), ())), preferred_elem...  25 us
    psum x1, blocking collectives, body(): lax.psum((first_gradient_sum, second_gradient_sum, class_tile), 'rep')  21.3 us
    another operation x1, local copies, waits for them, and re-layouts, body(): jnp.stack(parts_list, 1)  19 us
  transfers between devices with their start and end apart: 3, of which 3 were waited for; matrix products, arithmetic and copies ran while one was open for 21% of the time, Pallas kernels for 0%

profile of v1, /device:TPU:0, one launch (start us, length us, event | category | flops | bytes accessed | tf_op | source)
XLA Modules:
  0.0 404.4 jit_solution(14716452994521681616)
XLA Ops:
  8.7 6.0 %all-gather.1 = f32[4,1,256]{2,1,0:T(1,128)S(1)} all-gather(f32[1,1,256]{2,1,0:T(1,128)S(1)} %bitcast.176), channel_id=2, replica_groups=mesh['rep'=8,'tile'=4] {'tile'}, dimensions={0}, use_global_device_ids=true | all-gather | bytes 5120 | tf_op jit(solution)/shard_map/all_gather | solution.py:44
  16.2 7.6 %psum.63 = f32[256]{0:T(256)S(1)} all-reduce(f32[256]{0:T(256)S(1)} %multiply_reduce_fusion.1), channel_id=1, replica_groups=mesh['rep'=8,'tile'=4] {'tile'}, use_global_device_ids=true, to_apply=%region_3.0 | all-reduce | flops 256 | bytes 2048 | tf_op jit(solution)/shard_map/psum | solution.py:46
  27.3 2.5 fusion.63
  31.0 39.8 %all-reduce.1 = (f32[]{:T(128)}, f32[]{:T(128)}) all-reduce(f32[]{:T(128)} %get-tuple-element.31, f32[]{:T(128)} %get-tuple-element.40), channel_id=1, replica_groups=mesh['rep'=8,'tile'=4] {'rep','tile'}, use_global_device_ids=true, to_apply=%region_6.0 | all-reduce | flops 2 | bytes 16 | tf_op jit(solution)/shard_map/psum | solution.py:59
  72.5 4.6 %fusion.61 = (f32[256]{0:T(256)S(1)}, f32[256]{0:T(256)S(1)}, f32[1728,256]{1,0:T(8,128)}) fusion(f32[256]{0:T(256)S(1)} %get-tuple-element.49, f32[256]{0:T(256)S(1)} %broadcast_multiply_fusion.1, bf16[2,12,72,256]{3,2,1,0:T(8,128)(2,1)} %param.9, f32[3,256]{1,0:T(4,128)S(1)} %copy-done, f32[1728,3]{0,1:T(4,128)S(1)} %get-tuple-element.51, ...), kind=kOutput, calls=%fused_computation.92 | convolution fusion | flops 20374336 | bytes 4474368 | tf_op jit(solution)/shard_map/dot_general | solution.py:67
  77.1 6.9 %all-reduce.3 = (f32[256]{0:T(256)S(1)}, f32[256]{0:T(256)S(1)}, f32[3,256]{1,0:T(4,128)S(1)}) all-reduce(f32[256]{0:T(256)S(1)} %get-tuple-element.25, f32[256]{0:T(256)S(1)} %get-tuple-element.24, f32[3,256]{1,0:T(4,128)S(1)} %fusion.16), channel_id=1, replica_groups=mesh['rep'=8,'tile'=4] {'tile'}, use_global_device_ids=true, to_apply=%region_12.13 | all-reduce | flops 1280 | bytes 10240 | tf_op jit(solution)/shard_map/psum | solution.py:69
  83.9 2.3 multiply_convert_fusion
  86.3 1.5 collective-permute-start
  89.8 3.8 collective-permute-done.1
  93.6 1.8 fusion.5
  95.5 2.8 fusion.14
  98.3 2.8 fusion.13
  101.1 2.8 fusion.12
  103.9 2.8 fusion.11
  106.6 2.8 fusion.10
  109.4 2.8 fusion.9
  112.2 2.7 fusion.8
  114.9 2.8 fusion.7
  117.7 2.8 fusion.6
  120.5 19.0 %copy.18 = f32[1536,9,256]{2,1,0:T(8,128)} copy(f32[1536,9,256]{0,2,1:T(8,128)} %fusion.6) | data formatting | bytes 28311552 | tf_op jit(solution)/shard_map/stack | solution.py:117
  140.1 21.3 %all-reduce.2 = (f32[256]{0:T(256)}, f32[256]{0:T(256)}, f32[3,256]{1,0:T(4,128)}) all-reduce(f32[256]{0:T(256)S(1)} %get-tuple-element.37, f32[256]{0:T(256)S(1)} %get-tuple-element.38, f32[3,256]{1,0:T(4,128)S(1)} %get-tuple-element.39), channel_id=1, replica_groups=mesh['rep'=8,'tile'=4] {'rep'}, use_global_device_ids=true, to_apply=%region_14.15 | all-reduce | flops 1280 | bytes 10240 | tf_op jit(solution)/shard_map/psum | solution.py:77
  161.4 7.7 %fusion.33 = f32[1728,1536]{1,0:T(8,128)} fusion(bf16[1728,256]{1,0:T(8,128)(2,1)S(1)} %multiply_convert_fusion, bf16[9,1536,256]{2,1,0:T(8,128)(2,1)} %param.10), kind=kOutput, calls=%fused_computation.52 | convolution fusion | flops 1358954496 | bytes 12288000 | tf_op jit(solution)/shard_map/dot_general | solution.py:102
  169.8 8.2 %fusion.26 = f32[1728,1536]{1,0:T(8,128)} fusion(bf16[1728,256]{1,0:T(8,128)(2,1)S(1)} %bitcast.175, bf16[9,1536,256]{2,1,0:T(8,128)(2,1)} %param.10), kind=kOutput, calls=%fused_computation.45 | convolution fusion | flops 1358954496 | bytes 12288000 | tf_op jit(solution)/shard_map/dot_general | solution.py:102
  177.9 6.4 %fusion.29 = f32[1728,1536]{1,0:T(8,128)} fusion(bf16[1728,256]{1,0:T(8,128)(2,1)S(1)} %bitcast.174, bf16[9,1536,256]{2,1,0:T(8,128)(2,1)S(1)} %bitcast.168), kind=kOutput, calls=%fused_computation.48 | convolution fusion | flops 1358954496 | bytes 12288000 | tf_op jit(solution)/shard_map/dot_general | solution.py:102
  184.3 6.3 %fusion.31 = f32[1728,1536]{1,0:T(8,128)} fusion(bf16[1728,256]{1,0:T(8,128)(2,1)S(1)} %bitcast.173, bf16[9,1536,256]{2,1,0:T(8,128)(2,1)S(1)} %bitcast.168), kind=kOutput, calls=%fused_computation.50 | convolution fusion | flops 1358954496 | bytes 12288000 | tf_op jit(solution)/shard_map/dot_general | solution.py:102
  190.7 6.3 %fusion.35 = f32[1728,1536]{1,0:T(8,128)} fusion(bf16[1728,256]{1,0:T(8,128)(2,1)S(1)} %bitcast.172, bf16[9,1536,256]{2,1,0:T(8,128)(2,1)S(1)} %bitcast.168), kind=kOutput, calls=%fused_computation.54 | convolution fusion | flops 1358954496 | bytes 12288000 | tf_op jit(solution)/shard_map/dot_general | solution.py:102
  197.0 5.7 %fusion.37 = f32[1728,1536]{1,0:T(8,128)} fusion(bf16[1728,256]{1,0:T(8,128)(2,1)S(1)} %bitcast.171, bf16[9,1536,256]{2,1,0:T(8,128)(2,1)S(1)} %bitcast.168), kind=kOutput, calls=%fused_computation.56 | convolution fusion | flops 1358954496 | bytes 12288000 | tf_op jit(solution)/shard_map/dot_general | solution.py:102
  202.7 5.6 %fusion.41 = f32[1728,1536]{1,0:T(8,128)} fusion(bf16[1728,256]{1,0:T(8,128)(2,1)S(1)} %bitcast.170, bf16[9,1536,256]{2,1,0:T(8,128)(2,1)S(1)} %bitcast.168), kind=kOutput, calls=%fused_computation.60 | convolution fusion | flops 1358954496 | bytes 12288000 | tf_op jit(solution)/shard_map/dot_general | solution.py:102
  208.4 6.2 %fusion.39 = f32[1728,1536]{1,0:T(8,128)} fusion(bf16[1728,256]{1,0:T(8,128)(2,1)S(1)} %bitcast.165, bf16[9,1536,256]{2,1,0:T(8,128)(2,1)S(1)} %bitcast.168), kind=kOutput, calls=%fused_computation.58 | convolution fusion | flops 1358954496 | bytes 12288000 | tf_op jit(solution)/shard_map/dot_general | solution.py:102
  214.6 30.0 %add_convert_fusion = bf16[1728,1536]{1,0:T(8,128)(2,1)} fusion(f32[1728,1536]{1,0:T(8,128)} %fusion.26, f32[1728,1536]{1,0:T(8,128)} %fusion.29, f32[1728,1536]{1,0:T(8,128)} %fusion.31, f32[1728,1536]{1,0:T(8,128)} %fusion.33, f32[1728,1536]{1,0:T(8,128)} %fusion.35, f32[1728,1536]{1,0:T(8,128)} %fusion.37, f32[1728,1536]{1,0:T(8,128)} %fusion.41, ...), kind=kOutput, calls=%fused_computation.2 | convolution fusion | flops 1382842368 | bytes 91914240 | tf_op jit(solution)/shard_map/dot_general | solution.py:102
  244.6 149.6 %reduce-scatter.2.cloned.1.call-done = f32[48,9,256]{2,1,0:T(8,128)} async-done(((f32[1536,9,256]{2,1,0:T(8,128)}), f32[48,9,256]{2,1,0:T(8,128)}) %reduce-scatter.2.cloned.1.call-update) | async-done | bytes 442384 | tf_op jit(solution)/shard_map/reduce_scatter | solution.py:116
  394.2 2.2 copy.19
  (45 shorter events, 11.4 us)
Async XLA Ops:
  7.2 20.1 %copy-start = (f32[3,256]{1,0:T(4,128)S(1)}, f32[3,256]{1,0:T(4,128)}, u32[]{:S(2)}) copy-start(f32[3,256]{1,0:T(4,128)} %param.13) | copy-start | bytes 9220
  7.2 64.3 %copy-start.6 = (f32[256]{0:T(256)S(1)}, f32[256]{0:T(256)}, u32[]{:S(2)}) copy-start(f32[256]{0:T(256)} %param.11) | copy-start | bytes 3076
  7.2 64.3 %copy-start.7 = (f32[256]{0:T(256)S(1)}, f32[256]{0:T(256)}, u32[]{:S(2)}) copy-start(f32[256]{0:T(256)} %param.12) | copy-start | bytes 3076
  7.2 387.0 %reduce-scatter.2.cloned.1.call-start = ((), (), s32[]{:S(2)}) async-start(), calls=%async_computation.1 | async-start | bytes 25952256 | tf_op jit(solution)/shard_map/reduce_scatter | solution.py:116
  72.5 23.0 %slice-start = ((s8[5308416]{0:T(1024)(128)(4,1)}), s8[1114112]{0:T(1024)(128)(4,1)S(1)}, s32[]{:S(2)}) async-start(s8[5308416]{0:T(1024)(128)(4,1)} %bitcast.159), calls=%async_computation.2 | async-start | bytes 2228224
  83.9 11.5 %slice-start.1 = ((s8[5308416]{0:T(1024)(128)(4,1)}), s8[4194304]{0:T(1024)(128)(4,1)S(1)}, s32[]{:S(2)}) async-start(s8[5308416]{0:T(1024)(128)(4,1)} %bitcast.159), calls=%async_computation.3 | async-start | bytes 8388608
  86.3 3.5 collective-permute-start
  87.8 5.8 %collective-permute-start.1 = (bf16[2,12,72,256]{3,2,1,0:T(8,128)(2,1)S(1)}, bf16[2,12,72,256]{3,2,1,0:T(8,128)(2,1)S(1)}, u32[]{:S(2)}, u32[]{:S(2)}) collective-permute-start(bf16[2,12,72,256]{3,2,1,0:T(8,128)(2,1)S(1)} %bitcast.162), channel_id=1, source_target_pairs={{1,0},{2,1},{3,2},{5,4},{6,5},{7,6},{9,8},{10,9},{11,10},{13,12},{... | collective-permute-start | bytes 2654216 | tf_op jit(solution)/shard_map/ppermute | solution.py:21
  89.8 25.1 %copy-start.4 = (bf16[2,12,72,256]{3,2,1,0:T(8,128)(2,1)}, bf16[2,12,72,256]{3,2,1,0:T(8,128)(2,1)S(1)}, u32[]{:S(2)}) copy-start(bf16[2,12,72,256]{3,2,1,0:T(8,128)(2,1)S(1)} %collective-permute-done) | copy-start | bytes 2654212
  95.5 22.2 %copy-start.2 = (bf16[2,36,96,256]{3,2,1,0:T(8,128)(2,1)}, bf16[2,36,96,256]{3,2,1,0:T(8,128)(2,1)S(1)}, u32[]{:S(2)}) copy-start(bf16[2,36,96,256]{3,2,1,0:T(8,128)(2,1)S(1)} %fusion.5) | copy-start | bytes 10616836
  161.4 7.7 %copy-start.3 = (bf16[2,36,96,256]{3,2,1,0:T(8,128)(2,1)S(1)}, bf16[2,36,96,256]{3,2,1,0:T(8,128)(2,1)}, u32[]{:S(2)}) copy-start(bf16[2,36,96,256]{3,2,1,0:T(8,128)(2,1)} %copy-done.2) | copy-start | bytes 10616836
  169.1 8.8 %slice-start.2 = ((s8[7077888]{0:T(1024)(128)(4,1)}), s8[2883584]{0:T(1024)(128)(4,1)S(1)}, s32[]{:S(2)}) async-start(s8[7077888]{0:T(1024)(128)(4,1)} %bitcast.167), calls=%async_computation.4 | async-start | bytes 5767168
  169.7 8.2 %slice-start.3 = ((s8[7077888]{0:T(1024)(128)(4,1)}), s8[4194304]{0:T(1024)(128)(4,1)S(1)}, s32[]{:S(2)}) async-start(s8[7077888]{0:T(1024)(128)(4,1)} %bitcast.167), calls=%async_computation.5 | async-start | bytes 8388608
  208.4 6.2 %copy-start.5 = (bf16[2,12,72,256]{3,2,1,0:T(8,128)(2,1)S(1)}, bf16[2,12,72,256]{3,2,1,0:T(8,128)(2,1)}, u32[]{:S(2)}) copy-start(bf16[2,12,72,256]{3,2,1,0:T(8,128)(2,1)} %copy-done.4) | copy-start | bytes 2654212
  214.6 181.8 %copy-start.1 = (f32[3,256]{1,0:T(4,128)S(1)}, f32[3,256]{1,0:T(4,128)}, u32[]{:S(2)}) copy-start(f32[3,256]{1,0:T(4,128)} %param.13) | copy-start | bytes 9220
Sparse Core Ops, SparseCore 0:
  139.6 254.6 reduce-scatter.1
